TPU v7x, 128 devices: a whole 4x4x4 slice. The times are simulated.
128 devices in a mesh: grp: 16 (over y, z), lag: 8 (over x, core).
Axes of the slice: x: 4, y: 4, z: 4, core: 2. Of those that a mesh axis runs over, the one named last changes fastest.
Arguments:
- history: float32 [16, 512, 32, 128], P('lag', 'grp'), may hold values from -6 to 6
- tiles: bfloat16 [65536, 128, 128], P(('grp', 'lag')), may hold values from -0.01171875 to 0.01171875
- tile_src: int32 [65536], P(('grp', 'lag')), may hold values from 0 to 511
- tile_obs: int32 [65536], P(('grp', 'lag')), may hold values from 0 to 32
- tile_lag: int32 [65536], P(('grp', 'lag')), may hold values from 0 to 1
- incident: float32 [32, 32, 128], P('grp', 'lag'), may hold values from -6 to 6
- near_inverse: bfloat16 [32, 128, 128], P('grp'), may hold values from -0.5 to 0.5
Outputs:
- field: float32 [32, 32, 128], P('grp', 'lag')
- new_current: float32 [32, 32, 128], P('grp', 'lag')
Inputs may be any that keep to these rules, and one draw needn't show every extreme that they name: `tile_obs`: a value of 32 marks a padded tile.
All inputs are finite; a program needn't handle non-finite values.
Results may differ from a plain program's by a relative error of at most 0.0035.
Values may be sent and summed in bfloat16 or wider, within the bound.
No kernel may reach another device: no remote copies, remote signals or barrier semaphores. Data moves between devices by JAX's collectives and lax.ppermute only.
A program may use at most 128 MiB of HBM per device.

v0:
```python
import jax
import jax.numpy as jnp
from jax import lax
from jax.sharding import PartitionSpec as P

OBS_DEV = 2


def body(history, tiles, tile_src, tile_obs, tile_lag, incident, near_inverse):
    hist16 = history.astype(jnp.bfloat16)
    gathered = lax.all_gather(hist16, "grp", axis=1, tiled=True)
    lag_count = gathered.shape[0]
    source_count = gathered.shape[1]
    flat = gathered.reshape(lag_count * source_count, gathered.shape[2], gathered.shape[3])
    picked = flat[tile_lag * source_count + tile_src]
    terms = jnp.einsum("kas,kos->kao", picked, tiles, preferred_element_type=jnp.float32)
    observers = OBS_DEV * lax.axis_size("grp")
    partial_field = jax.ops.segment_sum(terms, tile_obs, num_segments=observers)
    angle_part = incident.shape[1]
    summed = lax.psum(partial_field, "lag")
    mine = lax.psum_scatter(summed, "grp", scatter_dimension=0, tiled=True)
    field = lax.dynamic_slice_in_dim(mine, lax.axis_index("lag") * angle_part, angle_part, 1)
    rhs = (incident - field).astype(jnp.bfloat16)
    new_current = jnp.einsum("oag,ohg->oah", rhs, near_inverse, preferred_element_type=jnp.float32)
    return (field, new_current)


def solution(mesh):
    return jax.shard_map(
        body,
        mesh=mesh,
        in_specs=(
            P("lag", "grp", None, None),
            P(("grp", "lag"), None, None),
            P(("grp", "lag")),
            P(("grp", "lag")),
            P(("grp", "lag")),
            P("grp", "lag", None),
            P("grp", None, None),
        ),
        out_specs=(P("grp", "lag", None), P("grp", "lag", None)),
        check_vma=False,
    )
```

profile of v0, /device:TPU:0, one launch (start us, length us, event | category | flops | bytes accessed | tf_op | source)
XLA Modules:
  0.0 255.2 jit_solution(2422170448194656881)
XLA Ops:
  7.2 0.0 copy-start
  7.2 0.0 all-gather.2.cloned.1.call-start
  7.2 2.2 convert_element_type.6
  9.4 0.0 all-gather.2.cloned.1.call-update
  9.4 0.0 reduce-scatter.2.cloned.1.call-start
  9.5 0.7 compare_select_fusion
  10.2 73.4 %all-gather.2.cloned.1.call-done = bf16[2,512,32,128]{3,2,1,0:T(8,128)(2,1)} async-done(((bf16[2,32,32,128]{3,2,1,0:T(8,128)(2,1)}), bf16[2,512,32,128]{3,2,1,0:T(8,128)(2,1)}) %all-gather.2.cloned.1.call-update) | async-done | bytes 8388624 | tf_op jit(solution)/shard_map/all_gather | solution.py:11
  83.6 6.5 %gather_fusion = bf16[512,32,128]{2,1,0:T(8,128)(2,1)} fusion(bf16[1024,32,128]{2,1,0:T(8,128)(2,1)} %bitcast.4, s32[1024]{0:T(1024)S(1)} %pad_clamp_fusion), kind=kCustom, calls=%fused_computation | custom fusion | bytes 8390656 | tf_op jit(solution)/shard_map/gather | solution.py:15
  90.1 0.0 copy-start.4
  90.1 15.0 %fusion.1 = f32[512,32,128]{2,1,0:T(8,128)} fusion(bf16[512,32,128]{2,1,0:T(8,128)(2,1)} %gather_fusion, bf16[512,128,128]{2,1,0:T(8,128)(2,1)} %param.8), kind=kOutput, calls=%fused_computation.7 | convolution fusion | flops 536870912 | bytes 29360128 | tf_op jit(solution)/shard_map/kas,kos->kao/dot_general | solution.py:16
  105.2 0.0 copy-done.4
  105.2 0.0 copy-start.3
  105.2 44.7 %scatter_fusion = f32[32,32,128]{2,1,0:T(8,128)S(1)} fusion(f32[32,32,128]{2,1,0:T(8,128)S(1)} %broadcast_in_dim.9, s32[512]{0:T(512)S(1)} %copy-done.4, f32[512,32,128]{2,1,0:T(8,128)} %fusion.1), kind=kCustom, calls=%fused_computation.1 | custom fusion | flops 2097152 | bytes 25167872 | tf_op jit(solution)/shard_map/scatter-add | solution.py:18
  149.9 0.0 copy-start.1
  149.9 0.8 copy-done.1
  150.7 0.0 reduce-scatter.2.cloned.1.call-update
  150.7 72.3 %reduce-scatter.2.cloned.1.call-done = f32[2,32,128]{2,1,0:T(8,128)} async-done(((f32[32,32,128]{2,1,0:T(8,128)}), f32[2,32,128]{2,1,0:T(8,128)}) %reduce-scatter.2.cloned.1.call-update) | async-done | bytes 32784 | tf_op jit(solution)/shard_map/reduce_scatter | solution.py:21
  223.0 24.6 %psum.8 = f32[2,32,128]{2,1,0:T(8,128)S(1)} all-reduce(f32[2,32,128]{2,1,0:T(8,128)} %reduce-scatter.2.cloned.1.call-done), channel_id=1, replica_groups=mesh['grp'=16,'lag'=8] {'lag'}, use_global_device_ids=true, to_apply=%region_1.0 | all-reduce | flops 8192 | bytes 65536 | tf_op jit(solution)/shard_map/psum | solution.py:20
  247.6 0.0 copy-done
  247.6 0.0 copy-done.3
  247.6 0.0 copy-start.2
  247.6 0.7 fusion
  248.4 0.0 copy-done.2
  (3 shorter events, 0.1 us)
Async XLA Ops:
  7.2 240.4 %copy-start = (bf16[2,128,128]{2,1,0:T(8,128)(2,1)S(1)}, bf16[2,128,128]{2,1,0:T(8,128)(2,1)}, u32[]{:S(2)}) copy-start(bf16[2,128,128]{2,1,0:T(8,128)(2,1)} %param.13) | copy-start | bytes 196612
  7.2 76.4 %all-gather.2.cloned.1.call-start = ((), (), s32[]{:S(2)}) async-start(), calls=%async_computation.1 | async-start | bytes 8912896 | tf_op jit(solution)/shard_map/all_gather | solution.py:11
  9.4 213.6 %reduce-scatter.2.cloned.1.call-start = ((), (), s32[]{:S(2)}) async-start(), calls=%async_computation.2 | async-start | bytes 557056 | tf_op jit(solution)/shard_map/reduce_scatter | solution.py:21
  90.1 15.0 %copy-start.4 = (s32[512]{0:T(512)S(1)}, s32[512]{0:T(512)}, u32[]{:S(2)}) copy-start(s32[512]{0:T(512)} %param.10) | copy-start | bytes 6148
  105.2 142.4 %copy-start.3 = (f32[2,4,128]{2,1,0:T(4,128)S(1)}, f32[2,4,128]{2,1,0:T(4,128)}, u32[]{:S(2)}) copy-start(f32[2,4,128]{2,1,0:T(4,128)} %param.12) | copy-start | bytes 12292
  149.9 0.8 copy-start.1
  247.6 0.8 copy-start.2
Sparse Core Ops, SparseCore 0:
  10.2 73.3 all-gather.1
  150.8 72.1 reduce-scatter.1
where the time goes:
time: 256 us; the launch traced here: 255 us
  waiting for transfers between devices  146 us (57%)
  other arithmetic  47.6 us (19%)
  blocking collectives  24.6 us (10%)
  matrix products  15.7 us (6%)
  between operations  14.1 us (6%)
  local copies, waits for them, and re-layouts  7.41 us (3%)
    all_gather x1, waiting for transfers between devices, body(): gathered = lax.all_gather(hist16, 'grp', axis=1, tiled=True)  73.4 us
    reduce_scatter x1, waiting for transfers between devices, body(): mine = lax.psum_scatter(summed, 'grp', scatter_dimension=0, tiled=True)  72.3 us
    scatter-add x1, other arithmetic, body(): partial_field = jax.ops.segment_sum(terms, tile_obs, num_segments=observers)  44.7 us
    psum x1, blocking collectives, body(): summed = lax.psum(partial_field, 'lag')  24.6 us
    dot_general x1, matrix products, body(): jnp.einsum('kas,kos->kao', picked, tiles, preferred_element_type=jnp.floa...  15 us
    gather x1, local copies, waits for them, and re-layouts, body(): picked = flat[tile_lag * source_count + tile_src]  6.55 us
  transfers between devices with their start and end apart: 2, of which 2 were waited for; matrix products, arithmetic and copies ran while one was open for 0% of the time, Pallas kernels for 0%

commit v1 on v0

--- a/solution.py
+++ b/solution.py
@@ -8,7 +8,12 @@
 
 def body(history, tiles, tile_src, tile_obs, tile_lag, incident, near_inverse):
     hist16 = history.astype(jnp.bfloat16)
-    gathered = lax.all_gather(hist16, "grp", axis=1, tiled=True)
+    ring = [hist16]
+    for hop in range(15):
+        ring.append(lax.ppermute(ring[-1], "grp", [(dev, (dev + 1) % 16) for dev in range(16)]))
+    gathered = jnp.roll(
+        jnp.concatenate(ring[::-1], axis=1), (lax.axis_index("grp") + 1) * ring[0].shape[1], axis=1
+    )
     lag_count = gathered.shape[0]
     source_count = gathered.shape[1]
     flat = gathered.reshape(lag_count * source_count, gathered.shape[2], gathered.shape[3])

time: 256 us -> 464 us (1.81)
  waiting for transfers between devices: 146 us -> 294 us
  local copies, waits for them, and re-layouts: 7.41 us -> 62.8 us
    ppermute x0 -> x15, waiting for transfers between devices: none -> 225 us  [body(): lax.ppermute(ring[-1], 'grp', [(dev, (dev + 1) % 16) for dev in range(16)])]
    all_gather x1 -> x0, waiting for transfers between devices: 73.4 us -> none  [body(): gathered = lax.all_gather(hist16, 'grp', axis=1, tiled=True)]
    unnamed x10 -> x78, local copies, waits for them, and re-layouts: 0.81 us -> 48.1 us
    dynamic_slice x0 -> x1, local copies, waits for them, and re-layouts: none -> 8.1 us  [body(): jnp.roll(jnp.concatenate(ring[::-1], axis=1), (lax.axis_index('grp') + 1)...]
  transfers between devices with their start and end apart: 2 -> 16, of which waited for: 2 -> 16; matrix products, arithmetic and copies ran while one was open for 0% -> 0% of each run, Pallas kernels for 0% -> 0%
where the time goes in v1:
time: 464 us; the launch traced here: 462 us
  waiting for transfers between devices  294 us (63%)
  local copies, waits for them, and re-layouts  62.8 us (14%)
  other arithmetic  48.7 us (10%)
  blocking collectives  24.6 us (5%)
  matrix products  15.8 us (3%)
  between operations  14.2 us (3%)
    ppermute x15, waiting for transfers between devices, body(): lax.ppermute(ring[-1], 'grp', [(dev, (dev + 1) % 16) for dev in range(16)])  225 us
    reduce_scatter x1, waiting for transfers between devices, body(): mine = lax.psum_scatter(summed, 'grp', scatter_dimension=0, tiled=True)  68.9 us
    unnamed x78, local copies, waits for them, and re-layouts  48.1 us
    scatter-add x1, other arithmetic, body(): partial_field = jax.ops.segment_sum(terms, tile_obs, num_segments=observers)  44.7 us
    psum x1, blocking collectives, body(): summed = lax.psum(partial_field, 'lag')  24.6 us
    dot_general x1, matrix products, body(): jnp.einsum('kas,kos->kao', picked, tiles, preferred_element_type=jnp.floa...  15 us
  transfers between devices with their start and end apart: 16, of which 16 were waited for; matrix products, arithmetic and copies ran while one was open for 0% of the time, Pallas kernels for 0%

profile of v1, /device:TPU:0, one launch (start us, length us, event | category | flops | bytes accessed | tf_op | source)
XLA Modules:
  0.0 461.9 jit_solution(14060553345037501640)
XLA Ops:
  8.6 2.1 collective-permute-start
  10.7 16.5 %collective-permute-done = bf16[2,32,32,128]{3,2,1,0:T(8,128)(2,1)S(1)} collective-permute-done((bf16[2,32,32,128]{3,2,1,0:T(8,128)(2,1)S(1)}, bf16[2,32,32,128]{3,2,1,0:T(8,128)(2,1)S(1)}, u32[]{:S(2)}, u32[]{:S(2)}) %collective-permute-start) | collective-permute-done | bytes 524320 | tf_op jit(solution)/shard_map/ppermute | solution.py:13
  27.2 16.4 %collective-permute-done.1 = bf16[2,32,32,128]{3,2,1,0:T(8,128)(2,1)S(1)} collective-permute-done((bf16[2,32,32,128]{3,2,1,0:T(8,128)(2,1)S(1)}, bf16[2,32,32,128]{3,2,1,0:T(8,128)(2,1)S(1)}, u32[]{:S(2)}, u32[]{:S(2)}) %collective-permute-start.1) | collective-permute-done | bytes 524320 | tf_op jit(solution)/shard_map/ppermute | solution.py:13
  43.6 15.5 %collective-permute-done.2 = bf16[2,32,32,128]{3,2,1,0:T(8,128)(2,1)S(1)} collective-permute-done((bf16[2,32,32,128]{3,2,1,0:T(8,128)(2,1)S(1)}, bf16[2,32,32,128]{3,2,1,0:T(8,128)(2,1)S(1)}, u32[]{:S(2)}, u32[]{:S(2)}) %collective-permute-start.2) | collective-permute-done | bytes 524320 | tf_op jit(solution)/shard_map/ppermute | solution.py:13
  59.1 14.6 %collective-permute-done.3 = bf16[2,32,32,128]{3,2,1,0:T(8,128)(2,1)S(1)} collective-permute-done((bf16[2,32,32,128]{3,2,1,0:T(8,128)(2,1)S(1)}, bf16[2,32,32,128]{3,2,1,0:T(8,128)(2,1)S(1)}, u32[]{:S(2)}, u32[]{:S(2)}) %collective-permute-start.3) | collective-permute-done | bytes 524320 | tf_op jit(solution)/shard_map/ppermute | solution.py:13
  73.7 13.7 %collective-permute-done.4 = bf16[2,32,32,128]{3,2,1,0:T(8,128)(2,1)S(1)} collective-permute-done((bf16[2,32,32,128]{3,2,1,0:T(8,128)(2,1)S(1)}, bf16[2,32,32,128]{3,2,1,0:T(8,128)(2,1)S(1)}, u32[]{:S(2)}, u32[]{:S(2)}) %collective-permute-start.4) | collective-permute-done | bytes 524320 | tf_op jit(solution)/shard_map/ppermute | solution.py:13
  88.2 12.7 %collective-permute-done.5 = bf16[2,32,32,128]{3,2,1,0:T(8,128)(2,1)S(1)} collective-permute-done((bf16[2,32,32,128]{3,2,1,0:T(8,128)(2,1)S(1)}, bf16[2,32,32,128]{3,2,1,0:T(8,128)(2,1)S(1)}, u32[]{:S(2)}, u32[]{:S(2)}) %collective-permute-start.5) | collective-permute-done | bytes 524320 | tf_op jit(solution)/shard_map/ppermute | solution.py:13
  101.7 12.5 %collective-permute-done.6 = bf16[2,32,32,128]{3,2,1,0:T(8,128)(2,1)S(1)} collective-permute-done((bf16[2,32,32,128]{3,2,1,0:T(8,128)(2,1)S(1)}, bf16[2,32,32,128]{3,2,1,0:T(8,128)(2,1)S(1)}, u32[]{:S(2)}, u32[]{:S(2)}) %collective-permute-start.6) | collective-permute-done | bytes 524320 | tf_op jit(solution)/shard_map/ppermute | solution.py:13
  115.1 13.3 %collective-permute-done.7 = bf16[2,32,32,128]{3,2,1,0:T(8,128)(2,1)S(1)} collective-permute-done((bf16[2,32,32,128]{3,2,1,0:T(8,128)(2,1)S(1)}, bf16[2,32,32,128]{3,2,1,0:T(8,128)(2,1)S(1)}, u32[]{:S(2)}, u32[]{:S(2)}) %collective-permute-start.7) | collective-permute-done | bytes 524320 | tf_op jit(solution)/shard_map/ppermute | solution.py:13
  129.2 14.4 %collective-permute-done.8 = bf16[2,32,32,128]{3,2,1,0:T(8,128)(2,1)S(1)} collective-permute-done((bf16[2,32,32,128]{3,2,1,0:T(8,128)(2,1)S(1)}, bf16[2,32,32,128]{3,2,1,0:T(8,128)(2,1)S(1)}, u32[]{:S(2)}, u32[]{:S(2)}) %collective-permute-start.8) | collective-permute-done | bytes 524320 | tf_op jit(solution)/shard_map/ppermute | solution.py:13
  144.4 15.5 %collective-permute-done.9 = bf16[2,32,32,128]{3,2,1,0:T(8,128)(2,1)S(1)} collective-permute-done((bf16[2,32,32,128]{3,2,1,0:T(8,128)(2,1)S(1)}, bf16[2,32,32,128]{3,2,1,0:T(8,128)(2,1)S(1)}, u32[]{:S(2)}, u32[]{:S(2)}) %collective-permute-start.9) | collective-permute-done | bytes 524320 | tf_op jit(solution)/shard_map/ppermute | solution.py:13
  160.7 16.6 %collective-permute-done.10 = bf16[2,32,32,128]{3,2,1,0:T(8,128)(2,1)S(1)} collective-permute-done((bf16[2,32,32,128]{3,2,1,0:T(8,128)(2,1)S(1)}, bf16[2,32,32,128]{3,2,1,0:T(8,128)(2,1)S(1)}, u32[]{:S(2)}, u32[]{:S(2)}) %collective-permute-start.10) | collective-permute-done | bytes 524320 | tf_op jit(solution)/shard_map/ppermute | solution.py:13
  178.1 17.8 %collective-permute-done.11 = bf16[2,32,32,128]{3,2,1,0:T(8,128)(2,1)S(1)} collective-permute-done((bf16[2,32,32,128]{3,2,1,0:T(8,128)(2,1)S(1)}, bf16[2,32,32,128]{3,2,1,0:T(8,128)(2,1)S(1)}, u32[]{:S(2)}, u32[]{:S(2)}) %collective-permute-start.11) | collective-permute-done | bytes 524320 | tf_op jit(solution)/shard_map/ppermute | solution.py:13
  196.7 17.3 %collective-permute-done.12 = bf16[2,32,32,128]{3,2,1,0:T(8,128)(2,1)S(1)} collective-permute-done((bf16[2,32,32,128]{3,2,1,0:T(8,128)(2,1)S(1)}, bf16[2,32,32,128]{3,2,1,0:T(8,128)(2,1)S(1)}, u32[]{:S(2)}, u32[]{:S(2)}) %collective-permute-start.12) | collective-permute-done | bytes 524320 | tf_op jit(solution)/shard_map/ppermute | solution.py:13
  214.8 16.0 %collective-permute-done.13 = bf16[2,32,32,128]{3,2,1,0:T(8,128)(2,1)} collective-permute-done((bf16[2,32,32,128]{3,2,1,0:T(8,128)(2,1)S(1)}, bf16[2,32,32,128]{3,2,1,0:T(8,128)(2,1)}, u32[]{:S(2)}, u32[]{:S(2)}) %collective-permute-start.13) | collective-permute-done | bytes 524320 | tf_op jit(solution)/shard_map/ppermute | solution.py:13
  231.7 11.9 %collective-permute-done.14 = bf16[2,32,32,128]{3,2,1,0:T(8,128)(2,1)} collective-permute-done((bf16[2,32,32,128]{3,2,1,0:T(8,128)(2,1)}, bf16[2,32,32,128]{3,2,1,0:T(8,128)(2,1)}, u32[]{:S(2)}, u32[]{:S(2)}) %collective-permute-start.14) | collective-permute-done | bytes 524320 | tf_op jit(solution)/shard_map/ppermute | solution.py:13
  243.6 1.9 constant_dynamic-update-slice_fusion.31
  245.5 1.9 constant_dynamic-update-slice_fusion.30
  249.4 1.9 constant_dynamic-update-slice_fusion.28
  251.3 1.9 constant_dynamic-update-slice_fusion.27
  255.2 1.9 constant_dynamic-update-slice_fusion.25
  257.1 1.9 constant_dynamic-update-slice_fusion.24
  259.0 1.9 constant_dynamic-update-slice_fusion.23
  262.9 1.9 constant_dynamic-update-slice_fusion.21
  269.2 1.9 constant_dynamic-update-slice_fusion.15
  271.1 1.9 constant_dynamic-update-slice_fusion.14
  285.5 8.1 %constant_dynamic-slice_fusion.1 = bf16[2,512,32,128]{3,2,1,0:T(8,128)(2,1)} fusion(bf16[2,1024,32,128]{3,2,1,0:T(8,128)(2,1)} %constant_dynamic-update-slice_fusion, s32[]{:T(128)S(6)} %select_n.20), kind=kLoop, calls=%fused_computation.39 | loop fusion | bytes 16777220 | tf_op jit(solution)/shard_map/jit(_roll_dynamic)/dynamic_slice | solution.py:14
  293.5 6.6 %gather_fusion = bf16[512,32,128]{2,1,0:T(8,128)(2,1)} fusion(bf16[1024,32,128]{2,1,0:T(8,128)(2,1)} %bitcast.4, s32[1024]{0:T(1024)S(1)} %pad_clamp_fusion), kind=kCustom, calls=%fused_computation | custom fusion | bytes 8390656 | tf_op jit(solution)/shard_map/gather | solution.py:20
  300.1 15.0 %fusion.1 = f32[512,32,128]{2,1,0:T(8,128)} fusion(bf16[512,32,128]{2,1,0:T(8,128)(2,1)} %gather_fusion, bf16[512,128,128]{2,1,0:T(8,128)(2,1)} %param.8), kind=kOutput, calls=%fused_computation.40 | convolution fusion | flops 536870912 | bytes 29360128 | tf_op jit(solution)/shard_map/kas,kos->kao/dot_general | solution.py:21
  315.2 44.7 %scatter_fusion = f32[32,32,128]{2,1,0:T(8,128)S(1)} fusion(f32[32,32,128]{2,1,0:T(8,128)S(1)} %broadcast_in_dim.9, s32[512]{0:T(512)S(1)} %copy-done.23, f32[512,32,128]{2,1,0:T(8,128)} %fusion.1), kind=kCustom, calls=%fused_computation.1 | custom fusion | flops 2097152 | bytes 25167872 | tf_op jit(solution)/shard_map/scatter-add | solution.py:23
  360.7 68.9 %reduce-scatter.2.cloned.1.call-done = f32[2,32,128]{2,1,0:T(8,128)} async-done(((f32[32,32,128]{2,1,0:T(8,128)}), f32[2,32,128]{2,1,0:T(8,128)}) %reduce-scatter.2.cloned.1.call-update) | async-done | bytes 32784 | tf_op jit(solution)/shard_map/reduce_scatter | solution.py:26
  429.6 24.6 %psum.8 = f32[2,32,128]{2,1,0:T(8,128)S(1)} all-reduce(f32[2,32,128]{2,1,0:T(8,128)} %reduce-scatter.2.cloned.1.call-done), channel_id=1, replica_groups=mesh['grp'=16,'lag'=8] {'lag'}, use_global_device_ids=true, to_apply=%region_1.2 | all-reduce | flops 8192 | bytes 65536 | tf_op jit(solution)/shard_map/psum | solution.py:25
  (92 shorter events, 33.7 us)
Async XLA Ops:
  7.2 447.1 %copy-start = (bf16[2,128,128]{2,1,0:T(8,128)(2,1)S(1)}, bf16[2,128,128]{2,1,0:T(8,128)(2,1)}, u32[]{:S(2)}) copy-start(bf16[2,128,128]{2,1,0:T(8,128)(2,1)} %param.13) | copy-start | bytes 196612
  7.2 261.1 %copy-start.2 = (f32[2,32,32,128]{3,2,1,0:T(8,128)S(1)}, f32[2,32,32,128]{3,2,1,0:T(8,128)}, u32[]{:S(2)}) copy-start(f32[2,32,32,128]{3,2,1,0:T(8,128)} %param.7) | copy-start | bytes 3145732
  7.2 422.4 %reduce-scatter.2.cloned.1.call-start = ((), (), s32[]{:S(2)}) async-start(), calls=%async_computation.1 | async-start | bytes 557056 | tf_op jit(solution)/shard_map/reduce_scatter | solution.py:26
  8.6 18.6 %collective-permute-start = (bf16[2,32,32,128]{3,2,1,0:T(8,128)(2,1)S(1)}, bf16[2,32,32,128]{3,2,1,0:T(8,128)(2,1)S(1)}, u32[]{:S(2)}, u32[]{:S(2)}) collective-permute-start(bf16[2,32,32,128]{3,2,1,0:T(8,128)(2,1)S(1)} %convert_element_type.6), channel_id=1, source_target_pairs={{0,8},{8,16},{16,24},{24,32},{32,40},{40,48},{48,56},{56,64},{64,7... | collective-permute-start | bytes 1572872 | tf_op jit(solution)/shard_map/ppermute | solution.py:13
  27.2 16.4 %collective-permute-start.1 = (bf16[2,32,32,128]{3,2,1,0:T(8,128)(2,1)S(1)}, bf16[2,32,32,128]{3,2,1,0:T(8,128)(2,1)S(1)}, u32[]{:S(2)}, u32[]{:S(2)}) collective-permute-start(bf16[2,32,32,128]{3,2,1,0:T(8,128)(2,1)S(1)} %collective-permute-done), channel_id=1, source_target_pairs={{0,8},{8,16},{16,24},{24,32},{32,40},{40,48},{48,56},{56,64},{64,7... | collective-permute-start | bytes 1572872 | tf_op jit(solution)/shard_map/ppermute | solution.py:13
  43.6 15.5 %collective-permute-start.2 = (bf16[2,32,32,128]{3,2,1,0:T(8,128)(2,1)S(1)}, bf16[2,32,32,128]{3,2,1,0:T(8,128)(2,1)S(1)}, u32[]{:S(2)}, u32[]{:S(2)}) collective-permute-start(bf16[2,32,32,128]{3,2,1,0:T(8,128)(2,1)S(1)} %collective-permute-done.1), channel_id=1, source_target_pairs={{0,8},{8,16},{16,24},{24,32},{32,40},{40,48},{48,56},{56,64},{64,7... | collective-permute-start | bytes 1572872 | tf_op jit(solution)/shard_map/ppermute | solution.py:13
  59.1 14.6 %collective-permute-start.3 = (bf16[2,32,32,128]{3,2,1,0:T(8,128)(2,1)S(1)}, bf16[2,32,32,128]{3,2,1,0:T(8,128)(2,1)S(1)}, u32[]{:S(2)}, u32[]{:S(2)}) collective-permute-start(bf16[2,32,32,128]{3,2,1,0:T(8,128)(2,1)S(1)} %collective-permute-done.2), channel_id=1, source_target_pairs={{0,8},{8,16},{16,24},{24,32},{32,40},{40,48},{48,56},{56,64},{64,7... | collective-permute-start | bytes 1572872 | tf_op jit(solution)/shard_map/ppermute | solution.py:13
  73.7 13.7 %collective-permute-start.4 = (bf16[2,32,32,128]{3,2,1,0:T(8,128)(2,1)S(1)}, bf16[2,32,32,128]{3,2,1,0:T(8,128)(2,1)S(1)}, u32[]{:S(2)}, u32[]{:S(2)}) collective-permute-start(bf16[2,32,32,128]{3,2,1,0:T(8,128)(2,1)S(1)} %collective-permute-done.3), channel_id=1, source_target_pairs={{0,8},{8,16},{16,24},{24,32},{32,40},{40,48},{48,56},{56,64},{64,7... | collective-permute-start | bytes 1572872 | tf_op jit(solution)/shard_map/ppermute | solution.py:13
  88.2 12.7 %collective-permute-start.5 = (bf16[2,32,32,128]{3,2,1,0:T(8,128)(2,1)S(1)}, bf16[2,32,32,128]{3,2,1,0:T(8,128)(2,1)S(1)}, u32[]{:S(2)}, u32[]{:S(2)}) collective-permute-start(bf16[2,32,32,128]{3,2,1,0:T(8,128)(2,1)S(1)} %collective-permute-done.4), channel_id=1, source_target_pairs={{0,8},{8,16},{16,24},{24,32},{32,40},{40,48},{48,56},{56,64},{64,7... | collective-permute-start | bytes 1572872 | tf_op jit(solution)/shard_map/ppermute | solution.py:13
  101.7 12.5 %collective-permute-start.6 = (bf16[2,32,32,128]{3,2,1,0:T(8,128)(2,1)S(1)}, bf16[2,32,32,128]{3,2,1,0:T(8,128)(2,1)S(1)}, u32[]{:S(2)}, u32[]{:S(2)}) collective-permute-start(bf16[2,32,32,128]{3,2,1,0:T(8,128)(2,1)S(1)} %collective-permute-done.5), channel_id=1, source_target_pairs={{0,8},{8,16},{16,24},{24,32},{32,40},{40,48},{48,56},{56,64},{64,7... | collective-permute-start | bytes 1572872 | tf_op jit(solution)/shard_map/ppermute | solution.py:13
  114.2 0.8 copy-start.7
  115.0 13.4 %collective-permute-start.7 = (bf16[2,32,32,128]{3,2,1,0:T(8,128)(2,1)S(1)}, bf16[2,32,32,128]{3,2,1,0:T(8,128)(2,1)S(1)}, u32[]{:S(2)}, u32[]{:S(2)}) collective-permute-start(bf16[2,32,32,128]{3,2,1,0:T(8,128)(2,1)S(1)} %collective-permute-done.6), channel_id=1, source_target_pairs={{0,8},{8,16},{16,24},{24,32},{32,40},{40,48},{48,56},{56,64},{64,7... | collective-permute-start | bytes 1572872 | tf_op jit(solution)/shard_map/ppermute | solution.py:13
  129.2 14.4 %collective-permute-start.8 = (bf16[2,32,32,128]{3,2,1,0:T(8,128)(2,1)S(1)}, bf16[2,32,32,128]{3,2,1,0:T(8,128)(2,1)S(1)}, u32[]{:S(2)}, u32[]{:S(2)}) collective-permute-start(bf16[2,32,32,128]{3,2,1,0:T(8,128)(2,1)S(1)} %collective-permute-done.7), channel_id=1, source_target_pairs={{0,8},{8,16},{16,24},{24,32},{32,40},{40,48},{48,56},{56,64},{64,7... | collective-permute-start | bytes 1572872 | tf_op jit(solution)/shard_map/ppermute | solution.py:13
  143.6 0.8 copy-start.11
  144.4 15.5 %collective-permute-start.9 = (bf16[2,32,32,128]{3,2,1,0:T(8,128)(2,1)S(1)}, bf16[2,32,32,128]{3,2,1,0:T(8,128)(2,1)S(1)}, u32[]{:S(2)}, u32[]{:S(2)}) collective-permute-start(bf16[2,32,32,128]{3,2,1,0:T(8,128)(2,1)S(1)} %collective-permute-done.8), channel_id=1, source_target_pairs={{0,8},{8,16},{16,24},{24,32},{32,40},{40,48},{48,56},{56,64},{64,7... | collective-permute-start | bytes 1572872 | tf_op jit(solution)/shard_map/ppermute | solution.py:13
  160.7 16.6 %collective-permute-start.10 = (bf16[2,32,32,128]{3,2,1,0:T(8,128)(2,1)S(1)}, bf16[2,32,32,128]{3,2,1,0:T(8,128)(2,1)S(1)}, u32[]{:S(2)}, u32[]{:S(2)}) collective-permute-start(bf16[2,32,32,128]{3,2,1,0:T(8,128)(2,1)S(1)} %collective-permute-done.9), channel_id=1, source_target_pairs={{0,8},{8,16},{16,24},{24,32},{32,40},{40,48},{48,56},{56,64},{64,7... | collective-permute-start | bytes 1572872 | tf_op jit(solution)/shard_map/ppermute | solution.py:13
  178.1 17.8 %collective-permute-start.11 = (bf16[2,32,32,128]{3,2,1,0:T(8,128)(2,1)S(1)}, bf16[2,32,32,128]{3,2,1,0:T(8,128)(2,1)S(1)}, u32[]{:S(2)}, u32[]{:S(2)}) collective-permute-start(bf16[2,32,32,128]{3,2,1,0:T(8,128)(2,1)S(1)} %collective-permute-done.10), channel_id=1, source_target_pairs={{0,8},{8,16},{16,24},{24,32},{32,40},{40,48},{48,56},{56,64},{64,7... | collective-permute-start | bytes 1572872 | tf_op jit(solution)/shard_map/ppermute | solution.py:13
  196.7 17.3 %collective-permute-start.12 = (bf16[2,32,32,128]{3,2,1,0:T(8,128)(2,1)S(1)}, bf16[2,32,32,128]{3,2,1,0:T(8,128)(2,1)S(1)}, u32[]{:S(2)}, u32[]{:S(2)}) collective-permute-start(bf16[2,32,32,128]{3,2,1,0:T(8,128)(2,1)S(1)} %collective-permute-done.11), channel_id=1, source_target_pairs={{0,8},{8,16},{16,24},{24,32},{32,40},{40,48},{48,56},{56,64},{64,7... | collective-permute-start | bytes 1572872 | tf_op jit(solution)/shard_map/ppermute | solution.py:13
  214.0 0.8 copy-start.19
  214.8 16.0 %collective-permute-start.13 = (bf16[2,32,32,128]{3,2,1,0:T(8,128)(2,1)S(1)}, bf16[2,32,32,128]{3,2,1,0:T(8,128)(2,1)}, u32[]{:S(2)}, u32[]{:S(2)}) collective-permute-start(bf16[2,32,32,128]{3,2,1,0:T(8,128)(2,1)S(1)} %collective-permute-done.12), channel_id=1, source_target_pairs={{0,8},{8,16},{16,24},{24,32},{32,40},{40,48},{48,56},{56,64},{64,7... | collective-permute-start | bytes 1572872 | tf_op jit(solution)/shard_map/ppermute | solution.py:13
  230.8 12.8 %collective-permute-start.14 = (bf16[2,32,32,128]{3,2,1,0:T(8,128)(2,1)}, bf16[2,32,32,128]{3,2,1,0:T(8,128)(2,1)}, u32[]{:S(2)}, u32[]{:S(2)}) collective-permute-start(bf16[2,32,32,128]{3,2,1,0:T(8,128)(2,1)} %collective-permute-done.13), channel_id=1, source_target_pairs={{0,8},{8,16},{16,24},{24,32},{32,40},{40,48},{48,56},{56,64},{64,7... | collective-permute-start | bytes 1572872 | tf_op jit(solution)/shard_map/ppermute | solution.py:13
  230.8 42.3 %copy-start.20 = (bf16[2,32,32,128]{3,2,1,0:T(8,128)(2,1)S(1)}, bf16[2,32,32,128]{3,2,1,0:T(8,128)(2,1)}, u32[]{:S(2)}) copy-start(bf16[2,32,32,128]{3,2,1,0:T(8,128)(2,1)} %copy-done.19) | copy-start | bytes 1572868
  230.8 43.1 %copy-start.18 = (bf16[2,32,32,128]{3,2,1,0:T(8,128)(2,1)S(1)}, bf16[2,32,32,128]{3,2,1,0:T(8,128)(2,1)}, u32[]{:S(2)}) copy-start(bf16[2,32,32,128]{3,2,1,0:T(8,128)(2,1)} %copy-done.17) | copy-start | bytes 1572868
  230.8 44.0 %copy-start.16 = (bf16[2,32,32,128]{3,2,1,0:T(8,128)(2,1)S(1)}, bf16[2,32,32,128]{3,2,1,0:T(8,128)(2,1)}, u32[]{:S(2)}) copy-start(bf16[2,32,32,128]{3,2,1,0:T(8,128)(2,1)} %copy-done.15) | copy-start | bytes 1572868
  230.8 44.9 %copy-start.14 = (bf16[2,32,32,128]{3,2,1,0:T(8,128)(2,1)S(1)}, bf16[2,32,32,128]{3,2,1,0:T(8,128)(2,1)}, u32[]{:S(2)}) copy-start(bf16[2,32,32,128]{3,2,1,0:T(8,128)(2,1)} %copy-done.13) | copy-start | bytes 1572868
  230.8 45.8 %copy-start.12 = (bf16[2,32,32,128]{3,2,1,0:T(8,128)(2,1)S(1)}, bf16[2,32,32,128]{3,2,1,0:T(8,128)(2,1)}, u32[]{:S(2)}) copy-start(bf16[2,32,32,128]{3,2,1,0:T(8,128)(2,1)} %copy-done.11) | copy-start | bytes 1572868
  230.8 46.6 %copy-start.10 = (bf16[2,32,32,128]{3,2,1,0:T(8,128)(2,1)S(1)}, bf16[2,32,32,128]{3,2,1,0:T(8,128)(2,1)}, u32[]{:S(2)}) copy-start(bf16[2,32,32,128]{3,2,1,0:T(8,128)(2,1)} %copy-done.9) | copy-start | bytes 1572868
  230.8 47.5 %copy-start.8 = (bf16[2,32,32,128]{3,2,1,0:T(8,128)(2,1)S(1)}, bf16[2,32,32,128]{3,2,1,0:T(8,128)(2,1)}, u32[]{:S(2)}) copy-start(bf16[2,32,32,128]{3,2,1,0:T(8,128)(2,1)} %copy-done.7) | copy-start | bytes 1572868
  230.8 48.4 %copy-start.6 = (bf16[2,32,32,128]{3,2,1,0:T(8,128)(2,1)S(1)}, bf16[2,32,32,128]{3,2,1,0:T(8,128)(2,1)}, u32[]{:S(2)}) copy-start(bf16[2,32,32,128]{3,2,1,0:T(8,128)(2,1)} %copy-done.5) | copy-start | bytes 1572868
  230.9 49.3 %copy-start.4 = (bf16[2,32,32,128]{3,2,1,0:T(8,128)(2,1)S(1)}, bf16[2,32,32,128]{3,2,1,0:T(8,128)(2,1)}, u32[]{:S(2)}) copy-start(bf16[2,32,32,128]{3,2,1,0:T(8,128)(2,1)} %copy-done.3) | copy-start | bytes 1572868
  300.1 15.1 %copy-start.23 = (s32[512]{0:T(512)S(1)}, s32[512]{0:T(512)}, u32[]{:S(2)}) copy-start(s32[512]{0:T(512)} %param.10) | copy-start | bytes 6148
  315.2 139.1 %copy-start.22 = (f32[2,4,128]{2,1,0:T(4,128)S(1)}, f32[2,4,128]{2,1,0:T(4,128)}, u32[]{:S(2)}) copy-start(f32[2,4,128]{2,1,0:T(4,128)} %param.12) | copy-start | bytes 12292
  (8 other events, 6.3 us)
Sparse Core Ops, SparseCore 0:
  360.9 68.7 reduce-scatter.1
